TPU v7x, 256 devices: a whole 4x4x8 slice. The times are simulated.
256 devices in a mesh: row: 16 (over z, y_hi), col: 16 (over x, y_lo, core).
Axes of the slice: x: 4, y: 4 (y_hi: 2, y_lo: 2; y = y_hi * 2 + y_lo), z: 8, core: 2. Of those that a mesh axis runs over, the one named last changes fastest.
Arguments:
- queries: bfloat16 [32, 2048, 128], P('row', 'col'), may hold values from -6.5 to 6.5
- keys: bfloat16 [32, 2048, 128], P('row', 'col'), may hold values from -6.5 to 6.5
- values: bfloat16 [32, 2048, 128], P('row', 'col'), may hold values from -6 to 6
- gate: bfloat16 [32, 2048, 128], P('row', 'col'), may hold values from -6 to 6
- bias: bfloat16 [4, 2048, 2048], P(None, 'col'), may hold values from -7.5 to 7.5
- grad_out: bfloat16 [32, 2048, 128], P('row', 'col'), may hold values from -6 to 6
- block_mask: int32 [16, 16], replicated, may hold values from 0 to 1, as said below
Outputs:
- query_grad: bfloat16 [32, 2048, 128], P('row', 'col')
- key_grad: bfloat16 [32, 2048, 128], P('row', 'col')
- value_grad: bfloat16 [32, 2048, 128], P('row', 'col')
- gate_grad: bfloat16 [32, 2048, 128], P('row', 'col')
- bias_grad: float32 [4, 2048, 2048], P(None, 'col', 'row')
Inputs may be any that keep to these rules, and one draw needn't show every extreme that they name: `block_mask`: every diagonal block is 1.
All inputs are finite; a program needn't handle non-finite values.
Results may differ from a plain program's by a relative error of at most 0.02.
Values may be sent and summed in bfloat16 or wider, within the bound.
No kernel may reach another device: no remote copies, remote signals or barrier semaphores. Data moves between devices by JAX's collectives and lax.ppermute only.
A program may use at most 64 MiB of HBM per device.

v0:
```python
import math
import jax
import jax.numpy as jnp
from jax import lax
from jax.sharding import PartitionSpec as P

H = 4
DH = 32
BLK = 128
NEGATIVE = -1000000000.0


def block_flags(block_mask, first_row, row_count, key_block):
    block_ids = (first_row + jnp.arange(row_count, dtype=jnp.int32)) // BLK
    column = lax.dynamic_index_in_dim(block_mask, key_block, axis=1, keepdims=False)
    matching = block_ids[:, None] == jnp.arange(block_mask.shape[0], dtype=jnp.int32)[None, :]
    return jnp.sum(jnp.where(matching, column[None, :], 0), axis=1) > 0


def tile_scores(query_tile, key_tile, bias_tile, allowed, score_scale):
    products = jnp.einsum(
        "rjhd,rkhd->rhjk", query_tile, key_tile, preferred_element_type=jnp.float32
    )
    scores = products * score_scale + bias_tile.astype(jnp.float32)[None]
    return jnp.where(allowed[None, None, :, None], scores, NEGATIVE)


def tile_grads(
    query_tile, key_tile, value_tile, bias_tile, allowed, log_total, grad_dot, out_grad, score_scale
):
    scores = tile_scores(query_tile, key_tile, bias_tile, allowed, score_scale)
    weights = jnp.exp(scores - log_total[..., None])
    prob_grad = jnp.einsum(
        "rjhd,rkhd->rhjk", out_grad, value_tile, preferred_element_type=jnp.float32
    )
    return (weights, weights * (prob_grad - grad_dot[..., None]))


def local(queries, keys, values, gate, bias, grad_out, block_mask):
    slab_rows, local_cols, channels = queries.shape
    head_count = H
    head_size = DH
    score_scale = 1.0 / math.sqrt(head_size)
    col_start = lax.axis_index("col") * local_cols
    key_all, value_all = (
        lax.all_gather(keys, "col", axis=1, tiled=True),
        lax.all_gather(values, "col", axis=1, tiled=True),
    )
    all_cols = key_all.shape[1]
    blocks = all_cols // BLK
    query_heads = queries.reshape(slab_rows, local_cols, head_count, head_size)
    key_heads_all = key_all.reshape(slab_rows, all_cols, head_count, head_size)
    value_heads_all = value_all.reshape(slab_rows, all_cols, head_count, head_size)

    def key_slices(key_block):
        offset = key_block * BLK
        return (
            lax.dynamic_slice_in_dim(key_heads_all, offset, BLK, 1),
            lax.dynamic_slice_in_dim(value_heads_all, offset, BLK, 1),
            lax.dynamic_slice_in_dim(bias, offset, BLK, 2),
            block_flags(block_mask, col_start, local_cols, key_block),
        )

    def stats_step(key_block, carried):
        key_tile, value_tile, bias_tile, allowed = key_slices(key_block)

        def stats_update(state_in):
            row_top, row_mass = state_in
            scores = tile_scores(query_heads, key_tile, bias_tile, allowed, score_scale)
            new_top = jnp.maximum(row_top, jnp.max(scores, axis=3))
            row_mass = row_mass * jnp.exp(row_top - new_top) + jnp.sum(
                jnp.exp(scores - new_top[..., None]), axis=3
            )
            return (new_top, row_mass)

        return lax.cond(jnp.any(allowed), stats_update, lambda kept: kept, carried)

    stat_shape = (slab_rows, head_count, local_cols)
    row_top, row_mass = lax.fori_loop(
        0,
        blocks,
        stats_step,
        (jnp.full(stat_shape, -1e30, jnp.float32), jnp.zeros(stat_shape, jnp.float32)),
    )
    log_total = row_top + jnp.log(row_mass)

    def attend_step(key_block, carried):
        key_tile, value_tile, bias_tile, allowed = key_slices(key_block)

        def attend_update(running):
            scores = tile_scores(query_heads, key_tile, bias_tile, allowed, score_scale)
            probs = jnp.exp(scores - log_total[..., None]).astype(jnp.bfloat16)
            return running + jnp.einsum(
                "rhjk,rkhd->rjhd", probs, value_tile, preferred_element_type=jnp.float32
            )

        return lax.cond(jnp.any(allowed), attend_update, lambda kept: kept, carried)

    attended = lax.fori_loop(
        0,
        blocks,
        attend_step,
        jnp.zeros((slab_rows, local_cols, head_count, head_size), jnp.float32),
    )
    gate_sig = jax.nn.sigmoid(gate.astype(jnp.float32)).reshape(
        slab_rows, local_cols, head_count, head_size
    )
    cotangent = grad_out.astype(jnp.float32).reshape(slab_rows, local_cols, head_count, head_size)
    gate_grad = (
        (cotangent * attended * gate_sig * (1.0 - gate_sig))
        .astype(jnp.bfloat16)
        .reshape(slab_rows, local_cols, channels)
    )
    out_grad = (cotangent * gate_sig).astype(jnp.bfloat16)
    grad_dot = jnp.transpose(jnp.sum(out_grad.astype(jnp.float32) * attended, axis=3), (0, 2, 1))

    def grad_step(key_block, carried):
        key_tile, value_tile, bias_tile, allowed = key_slices(key_block)

        def grad_update(state_in):
            query_acc, bias_part, key_part, value_part = state_in
            weights, score_grad = tile_grads(
                query_heads,
                key_tile,
                value_tile,
                bias_tile,
                allowed,
                log_total,
                grad_dot,
                out_grad,
                score_scale,
            )
            score_grad_b = score_grad.astype(jnp.bfloat16)
            query_acc = query_acc + jnp.einsum(
                "rhjk,rkhd->rjhd", score_grad_b, key_tile, preferred_element_type=jnp.float32
            )
            offset = key_block * BLK
            bias_part = lax.dynamic_update_slice_in_dim(
                bias_part, jnp.sum(score_grad, axis=0), offset, 2
            )
            key_piece = jnp.einsum(
                "rhjk,rjhd->rkhd", score_grad_b, query_heads, preferred_element_type=jnp.float32
            )
            value_piece = jnp.einsum(
                "rhjk,rjhd->rkhd",
                weights.astype(jnp.bfloat16),
                out_grad,
                preferred_element_type=jnp.float32,
            )
            key_part = lax.dynamic_update_slice_in_dim(
                key_part, key_piece.reshape(slab_rows, BLK, channels), offset, 1
            )
            value_part = lax.dynamic_update_slice_in_dim(
                value_part, value_piece.reshape(slab_rows, BLK, channels), offset, 1
            )
            return (query_acc, bias_part, key_part, value_part)

        return lax.cond(jnp.any(allowed), grad_update, lambda kept: kept, carried)

    part_shape = (slab_rows, all_cols, channels)
    initial = (
        jnp.zeros((slab_rows, local_cols, head_count, head_size), jnp.float32),
        jnp.zeros((head_count, local_cols, all_cols), jnp.float32),
        jnp.zeros(part_shape, jnp.float32),
        jnp.zeros(part_shape, jnp.float32),
    )
    query_acc, bias_part, key_part, value_part = lax.fori_loop(0, blocks, grad_step, initial)
    key_sum, value_sum = (
        lax.psum_scatter(key_part, "col", scatter_dimension=1, tiled=True),
        lax.psum_scatter(value_part, "col", scatter_dimension=1, tiled=True),
    )
    key_grad = (key_sum * score_scale).astype(jnp.bfloat16)
    value_grad = value_sum.astype(jnp.bfloat16)
    bias_grad = lax.psum_scatter(bias_part, "row", scatter_dimension=2, tiled=True)
    query_grad = (
        (query_acc * score_scale).astype(jnp.bfloat16).reshape(slab_rows, local_cols, channels)
    )
    return (query_grad, key_grad, value_grad, gate_grad, bias_grad)


def solution(mesh):
    return jax.shard_map(
        local,
        mesh=mesh,
        in_specs=(
            P("row", "col", None),
            P("row", "col", None),
            P("row", "col", None),
            P("row", "col", None),
            P(None, "col", None),
            P("row", "col", None),
            P(),
        ),
        out_specs=(
            P("row", "col", None),
            P("row", "col", None),
            P("row", "col", None),
            P("row", "col", None),
            P(None, "col", "row"),
        ),
        check_vma=False,
    )
```

profile of v0, /device:TPU:4, one launch (start us, length us, event | category | flops | bytes accessed | tf_op | source)
XLA Modules:
  0.0 607.0 jit_solution(3435595489802957417)
XLA Ops:
  8.7 3.1 copy.84
  12.1 0.8 copy.80
  12.9 0.8 copy.79
  13.6 32.8 %all-gather.3.cloned.1.call-done = bf16[2,2048,128]{2,1,0:T(8,128)(2,1)} async-done(((bf16[2,128,128]{2,1,0:T(8,128)(2,1)}), bf16[2,2048,128]{2,1,0:T(8,128)(2,1)}) %all-gather.3.cloned.1.call-update) | async-done | bytes 1048592 | tf_op jit(solution)/shard_map/all_gather | solution.py:46
  46.5 1.5 copy.74
  48.0 26.1 %while.56 = (s32[]{:T(128)}, f32[2,4,128]{2,1,0:T(4,128)S(1)}, f32[2,4,128]{2,1,0:T(4,128)S(1)}, s32[]{:T(128)}, s32[16,16]{0,1:T(8,128)S(1)}, /*index=5*/bf16[2...) while((s32[]{:T(128)}, f32[2,4,128]{2,1,0:T(4,128)S(1)}, ...), condition=%wide.region_7.8_spmd, body=%wide.region_0.7_spmd.sunk | while | flops 9250950 | bytes 1891393 | solution.py:79
  74.1 9.0 %all-gather.5.cloned.1.call-done = bf16[2,2048,128]{2,1,0:T(8,128)(2,1)} async-done(((bf16[2,128,128]{2,1,0:T(8,128)(2,1)}), bf16[2,2048,128]{2,1,0:T(8,128)(2,1)}) %all-gather.5.cloned.1.call-update) | async-done | bytes 1048592 | tf_op jit(solution)/shard_map/all_gather | solution.py:47
  83.1 2.3 copy.78
  86.1 35.5 %while.57 = (s32[]{:T(128)}, f32[2,128,4,32]{1,3,2,0:T(8,128)}, s32[]{:T(128)}, s32[16,16]{0,1:T(8,128)S(1)}, bf16[2,2048,4,32]{1,3,2,0:T(8,128)(2,1)S(1)}, /*in...) while((s32[]{:T(128)}, f32[2,128,4,32]{1,3,2,0:T(8,128)}, ...), condition=%wide.region_13.14_spmd, body=%wide.region_8.13_spmd.sunk | while | flops 17539204 | bytes 1122349 | solution.py:99
  87.5 2.1 conditional.7
  87.5 2.1 fusion.14
  91.0 2.1 conditional.7
  91.0 2.1 fusion.14
  97.4 2.1 conditional.7
  97.4 2.1 fusion.14
  105.2 2.1 conditional.7
  105.3 2.1 fusion.14
  108.7 2.1 conditional.7
  108.8 2.1 fusion.14
  113.7 2.1 conditional.7
  113.7 2.1 fusion.14
  121.6 1.5 multiply_reduce_fusion
  123.1 2.2 broadcast_in_dim.201
  125.6 1.5 broadcast.279.clone
  127.1 50.5 %while.58 = (s32[]{:T(128)}, f32[2,128,4,32]{1,3,2,0:T(8,128)S(1)}, f32[4,128,2048]{1,2,0:T(8,128)}, f32[2,2048,128]{1,2,0:T(8,128)S(1)}, f32[2,2048,128]{1,2,0:...) while((s32[]{:T(128)}, f32[2,128,4,32]{1,3,2,0:T(8,128)S(1)}, ...), condition=%wide.region_21.22_spmd, body=%wide.region_15.21_spmd.sunk | while | flops 43163780 | bytes 5319889 | solution.py:167
  128.6 4.6 conditional.8
  128.6 0.9 dynamic-slice_convert_fusion.2
  129.9 1.2 fusion.49
  131.5 0.7 constant_dynamic-update-slice_fusion
  132.3 0.7 constant_dynamic-update-slice_fusion.2
  134.6 4.6 conditional.8
  134.6 0.9 dynamic-slice_convert_fusion.2
  135.9 1.2 fusion.49
  137.6 0.7 constant_dynamic-update-slice_fusion
  138.3 0.7 constant_dynamic-update-slice_fusion.2
  143.5 4.6 conditional.8
  143.6 0.9 dynamic-slice_convert_fusion.2
  144.8 1.2 fusion.49
  147.2 0.7 constant_dynamic-update-slice_fusion.2
  153.9 4.6 conditional.8
  153.9 0.9 dynamic-slice_convert_fusion.2
  155.2 1.2 fusion.49
  156.8 0.7 constant_dynamic-update-slice_fusion
  157.5 0.7 constant_dynamic-update-slice_fusion.2
  159.9 4.6 conditional.8
  159.9 0.9 dynamic-slice_convert_fusion.2
  161.2 1.2 fusion.49
  162.8 0.7 constant_dynamic-update-slice_fusion
  163.5 0.7 constant_dynamic-update-slice_fusion.2
  167.3 4.6 conditional.8
  167.4 0.9 dynamic-slice_convert_fusion.2
  168.6 1.2 fusion.49
  170.3 0.7 constant_dynamic-update-slice_fusion
  171.0 0.7 constant_dynamic-update-slice_fusion.2
  177.7 3.0 copy.86
  180.7 1.8 copy.85
  182.6 5.4 copy.87
  188.1 0.7 copy.88
  188.8 0.7 copy.89
  189.5 114.2 %reduce-scatter.6.cloned.1.call-done = f32[2,128,128]{2,1,0:T(8,128)} async-done(((f32[2,2048,128]{2,1,0:T(8,128)}), f32[2,128,128]{2,1,0:T(8,128)}) %reduce-scatter.6.cloned.1.call-update) | async-done | bytes 131088 | tf_op jit(solution)/shard_map/reduce_scatter | solution.py:170
  303.8 1.5 convert_element_type.99
  305.3 66.8 %reduce-scatter.4.cloned.1.call-done = f32[2,128,128]{2,1,0:T(8,128)} async-done(((f32[2,2048,128]{2,1,0:T(8,128)}), f32[2,128,128]{2,1,0:T(8,128)}) %reduce-scatter.4.cloned.1.call-update) | async-done | bytes 131088 | tf_op jit(solution)/shard_map/reduce_scatter | solution.py:169
  372.1 1.5 multiply_convert_fusion.1
  373.7 226.8 %reduce-scatter.8.cloned.1.call-done = f32[4,128,128]{2,1,0:T(8,128)} async-done(((f32[4,128,2048]{2,1,0:T(8,128)}), f32[4,128,128]{2,1,0:T(8,128)}) %reduce-scatter.8.cloned.1.call-update) | async-done | bytes 262160 | tf_op jit(solution)/shard_map/reduce_scatter | solution.py:174
  (325 shorter events, 51.5 us)
Async XLA Ops:
  7.2 39.3 %all-gather.3.cloned.1.call-start = ((), (), s32[]{:S(2)}) async-start(), calls=%async_computation.3 | async-start | bytes 1114112 | tf_op jit(solution)/shard_map/all_gather | solution.py:46
  7.9 75.2 %all-gather.5.cloned.1.call-start = ((), (), s32[]{:S(2)}) async-start(), calls=%async_computation.4 | async-start | bytes 1114112 | tf_op jit(solution)/shard_map/all_gather | solution.py:47
  8.7 295.1 %reduce-scatter.6.cloned.1.call-start = ((), (), s32[]{:S(2)}) async-start(), calls=%async_computation.6 | async-start | bytes 2228224 | tf_op jit(solution)/shard_map/reduce_scatter | solution.py:170
  8.7 3.1 copy-start.3
  8.7 3.3 copy-start.4
  8.7 3.3 copy-start.1
  8.7 4.1 copy-start.2
  121.6 1.6 copy-start
  180.7 191.4 %reduce-scatter.4.cloned.1.call-start = ((), (), s32[]{:S(2)}) async-start(), calls=%async_computation.5 | async-start | bytes 2228224 | tf_op jit(solution)/shard_map/reduce_scatter | solution.py:169
  182.6 417.9 %reduce-scatter.8.cloned.1.call-start = ((), (), s32[]{:S(2)}) async-start(), calls=%async_computation.7 | async-start | bytes 4456448 | tf_op jit(solution)/shard_map/reduce_scatter | solution.py:174
Sparse Core Ops, SparseCore 0:
  9.8 36.6 all-gather.2
  48.3 34.7 all-gather.4
  180.8 122.9 reduce-scatter.5
  306.2 65.8 reduce-scatter.3
  376.5 223.8 reduce-scatter.7
where the time goes:
time: 609 us; the launch traced here: 607 us
  waiting for transfers between devices  451 us (74%)
  other arithmetic  46.5 us (8%)
  local copies, waits for them, and re-layouts  34 us (6%)
  loops' own time  34 us (6%)
  matrix products  27.2 us (4%)
  between operations  13.9 us (2%)
    reduce_scatter x1, waiting for transfers between devices, local(): lax.psum_scatter(bias_part, 'row', scatter_dimension=2, tiled=True)  227 us
    reduce_scatter x1, waiting for transfers between devices, local(): lax.psum_scatter(value_part, 'col', scatter_dimension=1, tiled=True)  114 us
    reduce_scatter x1, waiting for transfers between devices, local(): lax.psum_scatter(key_part, 'col', scatter_dimension=1, tiled=True)  66.8 us
    all_gather x1, waiting for transfers between devices, local(): lax.all_gather(keys, 'col', axis=1, tiled=True)  32.8 us
    gt x48, other arithmetic, block_flags(): return jnp.sum(jnp.where(matching, column[None, :], 0), axis=1) > 0  30.5 us
    while x5, local copies, waits for them, and re-layouts, local(): lax.fori_loop(0, blocks, grad_step, initial)  13.3 us
    dot_general x6, matrix products, attend_update(): jnp.einsum('rhjk,rkhd->rjhd', probs, value_tile, preferred_element_type=j...  12.3 us
  transfers between devices with their start and end apart: 5, of which 5 were waited for; matrix products, arithmetic and copies ran while one was open for 5% of the time, Pallas kernels for 0%

commit v1 on v0

--- a/solution.py
+++ b/solution.py
@@ -42,8 +42,21 @@
     head_size = DH
     score_scale = 1.0 / math.sqrt(head_size)
     col_start = lax.axis_index("col") * local_cols
+
+    def show_positions(block_in, lane_axis):
+        oldest = jnp.concatenate(
+            lax.all_to_all(
+                jnp.stack(tuple((block_in for _ in range(lax.axis_size(lane_axis)))), 0),
+                split_axis=0,
+                axis_name=lane_axis,
+                concat_axis=0,
+            ),
+            1,
+        )
+        return oldest
+
     key_all, value_all = (
-        lax.all_gather(keys, "col", axis=1, tiled=True),
+        show_positions(keys, "col"),
         lax.all_gather(values, "col", axis=1, tiled=True),
     )
     all_cols = key_all.shape[1]

time: 609 us -> 590 us (0.969)
  waiting for transfers between devices: 451 us -> 422 us
    all_gather x1 -> x0, waiting for transfers between devices: 32.8 us -> none  [local(): lax.all_gather(keys, 'col', axis=1, tiled=True)]
    all_gather x1, waiting for transfers between devices: 9.01 us -> 0.02 us  [local(): lax.all_gather(values, 'col', axis=1, tiled=True)]
    all_to_all x0 -> x1, waiting for transfers between devices: none -> 8.46 us  [show_positions(): lax.all_to_all(jnp.stack(tuple((block_in for _ in range(lax.axis_size(lan...]
  transfers between devices with their start and end apart: 5 -> 5, of which waited for: 5 -> 4; matrix products, arithmetic and copies ran while one was open for 5% -> 6% of each run, Pallas kernels for 0% -> 0%
where the time goes in v1:
time: 590 us; the launch traced here: 588 us
  waiting for transfers between devices  422 us (72%)
  other arithmetic  46.5 us (8%)
  local copies, waits for them, and re-layouts  38 us (6%)
  loops' own time  34 us (6%)
  matrix products  27.2 us (5%)
  between operations  13.9 us (2%)
  starting transfers between devices  5.99 us (1%)
    reduce_scatter x1, waiting for transfers between devices, local(): lax.psum_scatter(bias_part, 'row', scatter_dimension=2, tiled=True)  227 us
    reduce_scatter x1, waiting for transfers between devices, local(): lax.psum_scatter(value_part, 'col', scatter_dimension=1, tiled=True)  120 us
    reduce_scatter x1, waiting for transfers between devices, local(): lax.psum_scatter(key_part, 'col', scatter_dimension=1, tiled=True)  66.5 us
    gt x48, other arithmetic, block_flags(): return jnp.sum(jnp.where(matching, column[None, :], 0), axis=1) > 0  30.5 us
    while x5, local copies, waits for them, and re-layouts, local(): lax.fori_loop(0, blocks, grad_step, initial)  13.3 us
    dot_general x6, matrix products, attend_update(): jnp.einsum('rhjk,rkhd->rjhd', probs, value_tile, preferred_element_type=j...  12.3 us
  transfers between devices with their start and end apart: 5, of which 4 were waited for; matrix products, arithmetic and copies ran while one was open for 6% of the time, Pallas kernels for 0%

profile of v1, /device:TPU:4, one launch (start us, length us, event | category | flops | bytes accessed | tf_op | source)
XLA Modules:
  0.0 587.9 jit_solution(86136132312958457)
XLA Ops:
  7.2 0.9 copy.95
  8.1 1.3 stack.2
  9.4 5.8 all-to-all-start
  16.1 3.1 copy.106
  19.4 0.8 copy.102
  20.2 0.8 copy.101
  20.9 8.5 %all-to-all-done = bf16[16,2,128,128]{2,3,1,0:T(8,128)(2,1)S(1)} async-done(((bf16[16,2,128,128]{2,3,1,0:T(8,128)(2,1)}), bf16[16,2,128,128]{2,3,1,0:T(8,128)(2,1)S(1)}, u32[]{:S(2)}, u32[]{:S(2)}) %all-to-all-start) | async-done | bytes 1048608 | tf_op jit(solution)/shard_map/all_to_all | solution.py:48
  29.4 1.7 copy.96
  31.1 1.5 reshape_reshape.3
  32.7 26.1 %while.56 = (s32[]{:T(128)}, f32[2,4,128]{2,1,0:T(4,128)S(1)}, f32[2,4,128]{2,1,0:T(4,128)S(1)}, s32[]{:T(128)}, s32[16,16]{0,1:T(8,128)S(1)}, /*index=5*/bf16[2...) while((s32[]{:T(128)}, f32[2,4,128]{2,1,0:T(4,128)S(1)}, ...), condition=%wide.region_7.8_spmd, body=%wide.region_0.7_spmd.sunk | while | flops 9250950 | bytes 1891393 | solution.py:92
  58.8 2.3 copy.100
  61.8 35.5 %while.57 = (s32[]{:T(128)}, f32[2,128,4,32]{1,3,2,0:T(8,128)}, s32[]{:T(128)}, s32[16,16]{0,1:T(8,128)S(1)}, bf16[2,2048,4,32]{1,3,2,0:T(8,128)(2,1)S(1)}, /*in...) while((s32[]{:T(128)}, f32[2,128,4,32]{1,3,2,0:T(8,128)}, ...), condition=%wide.region_13.14_spmd, body=%wide.region_8.13_spmd.sunk | while | flops 17539204 | bytes 1122349 | solution.py:112
  63.2 2.1 conditional.7
  63.2 2.1 fusion.14
  66.7 2.1 conditional.7
  66.8 2.1 fusion.14
  73.1 2.1 conditional.7
  73.1 2.1 fusion.14
  80.9 2.1 conditional.7
  81.0 2.1 fusion.14
  84.4 2.1 conditional.7
  84.5 2.1 fusion.14
  89.4 2.1 conditional.7
  89.5 2.1 fusion.14
  97.3 1.5 multiply_reduce_fusion
  98.8 2.2 broadcast_in_dim.201
  101.3 1.5 broadcast.281.clone
  102.9 50.5 %while.58 = (s32[]{:T(128)}, f32[2,128,4,32]{1,3,2,0:T(8,128)S(1)}, f32[4,128,2048]{1,2,0:T(8,128)}, f32[2,2048,128]{1,2,0:T(8,128)S(1)}, f32[2,2048,128]{1,2,0:...) while((s32[]{:T(128)}, f32[2,128,4,32]{1,3,2,0:T(8,128)S(1)}, ...), condition=%wide.region_21.22_spmd, body=%wide.region_15.21_spmd.sunk | while | flops 43163780 | bytes 5319889 | solution.py:180
  104.3 4.6 conditional.8
  104.3 0.9 dynamic-slice_convert_fusion.2
  105.6 1.2 fusion.49
  107.2 0.7 constant_dynamic-update-slice_fusion
  108.0 0.7 constant_dynamic-update-slice_fusion.2
  110.3 4.6 conditional.8
  110.3 0.9 dynamic-slice_convert_fusion.2
  111.6 1.2 fusion.49
  113.3 0.7 constant_dynamic-update-slice_fusion
  114.0 0.7 constant_dynamic-update-slice_fusion.2
  119.2 4.6 conditional.8
  119.3 0.9 dynamic-slice_convert_fusion.2
  120.5 1.2 fusion.49
  122.9 0.7 constant_dynamic-update-slice_fusion.2
  129.6 4.6 conditional.8
  129.6 0.9 dynamic-slice_convert_fusion.2
  130.9 1.2 fusion.49
  133.3 0.7 constant_dynamic-update-slice_fusion.2
  135.6 4.6 conditional.8
  135.6 0.9 dynamic-slice_convert_fusion.2
  136.9 1.2 fusion.49
  138.5 0.7 constant_dynamic-update-slice_fusion
  143.0 4.6 conditional.8
  143.1 0.9 dynamic-slice_convert_fusion.2
  144.3 1.2 fusion.49
  146.7 0.7 constant_dynamic-update-slice_fusion.2
  153.4 3.0 copy.108
  156.5 1.8 copy.107
  158.3 5.4 copy.109
  163.8 0.7 copy.110
  164.5 0.7 copy.111
  165.3 120.0 %reduce-scatter.6.cloned.1.call-done = f32[2,128,128]{2,1,0:T(8,128)} async-done(((f32[2,2048,128]{2,1,0:T(8,128)}), f32[2,128,128]{2,1,0:T(8,128)}) %reduce-scatter.6.cloned.1.call-update) | async-done | bytes 131088 | tf_op jit(solution)/shard_map/reduce_scatter | solution.py:183
  285.2 1.5 convert_element_type.99
  286.8 66.5 %reduce-scatter.4.cloned.1.call-done = f32[2,128,128]{2,1,0:T(8,128)} async-done(((f32[2,2048,128]{2,1,0:T(8,128)}), f32[2,128,128]{2,1,0:T(8,128)}) %reduce-scatter.4.cloned.1.call-update) | async-done | bytes 131088 | tf_op jit(solution)/shard_map/reduce_scatter | solution.py:182
  353.3 1.5 multiply_convert_fusion.1
  354.8 226.5 %reduce-scatter.8.cloned.1.call-done = f32[4,128,128]{2,1,0:T(8,128)} async-done(((f32[4,128,2048]{2,1,0:T(8,128)}), f32[4,128,128]{2,1,0:T(8,128)}) %reduce-scatter.8.cloned.1.call-update) | async-done | bytes 262160 | tf_op jit(solution)/shard_map/reduce_scatter | solution.py:187
  (327 shorter events, 52.9 us)
Async XLA Ops:
  9.4 20.0 %all-to-all-start = ((bf16[16,2,128,128]{2,3,1,0:T(8,128)(2,1)}), bf16[16,2,128,128]{2,3,1,0:T(8,128)(2,1)S(1)}, u32[]{:S(2)}, u32[]{:S(2)}) async-start(bf16[16,2,128,128]{2,3,1,0:T(8,128)(2,1)} %stack.2), calls=%async_computation | async-start | bytes 2097152 | tf_op jit(solution)/shard_map/all_to_all | solution.py:48
  15.2 43.5 %all-gather.2.cloned.1.call-start = ((), (), s32[]{:S(2)}) async-start(), calls=%async_computation.4 | async-start | bytes 1114112 | tf_op jit(solution)/shard_map/all_gather | solution.py:60
  16.0 269.3 %reduce-scatter.6.cloned.1.call-start = ((), (), s32[]{:S(2)}) async-start(), calls=%async_computation.6 | async-start | bytes 2228224 | tf_op jit(solution)/shard_map/reduce_scatter | solution.py:183
  16.0 3.1 copy-start.3
  16.0 3.3 copy-start.4
  16.0 3.3 copy-start.1
  16.1 4.1 copy-start.2
  97.3 1.6 copy-start
  156.4 196.9 %reduce-scatter.4.cloned.1.call-start = ((), (), s32[]{:S(2)}) async-start(), calls=%async_computation.5 | async-start | bytes 2228224 | tf_op jit(solution)/shard_map/reduce_scatter | solution.py:182
  158.3 423.1 %reduce-scatter.8.cloned.1.call-start = ((), (), s32[]{:S(2)}) async-start(), calls=%async_computation.7 | async-start | bytes 4456448 | tf_op jit(solution)/shard_map/reduce_scatter | solution.py:187
Sparse Core Ops, SparseCore 0:
  17.8 36.4 all-gather.1
  156.5 128.6 reduce-scatter.5
  287.8 65.4 reduce-scatter.3
  357.7 223.5 reduce-scatter.7
